TPU v7x, 256 devices: a whole 4x4x8 slice. The times are simulated.
256 devices in a mesh: own: 32 (over x, z), row: 8 (over y, core).
Axes of the slice: x: 4, y: 4, z: 8, core: 2. Of those that a mesh axis runs over, the one named last changes fastest.
Arguments:
- sigma_anc: float32 [16384, 16384], P('row', 'own'), may hold values from -1.5 to 1.5
- row_blocks: int32 [64, 8], replicated, may hold values from 0 to 63, as said below
- panel1: float32 [64, 2048, 256], P('own', 'row'), may hold values from -0.375 to 0.375
- diag_inv1: float32 [64, 256, 256], P('own'), as said below
- mask1: int32 [64, 8], P('own', 'row'), may hold values 0 or 1
- parent_block2: float32 [64, 256, 256], P('own'), may hold values from -0.375 to 0.375
- panel2: float32 [64, 2048, 256], P('own', 'row'), may hold values from -0.375 to 0.375
- diag_inv2: float32 [64, 256, 256], P('own'), as said below
- mask2: int32 [64, 8], P('own', 'row'), may hold values 0 or 1
Outputs:
- sel1_panel: float32 [64, 2048, 256], P('own', 'row')
- sel1_diag: float32 [64, 256, 256], P('own')
- sel2_parent: float32 [64, 256, 256], P('own')
- sel2_panel: float32 [64, 2048, 256], P('own', 'row')
- sel2_diag: float32 [64, 256, 256], P('own')
Inputs may be any that keep to these rules, and one draw needn't show every extreme that they name: `row_blocks`: entry l of each row lies in block rows 8 * l to 8 * (l + 1) - 1; for supernodes s with the same s // 2, the entries of one column l lie in different aligned runs of 2 block rows. `diag_inv1`: lower triangular, with diagonal entries from 1 to 2. `diag_inv2`: lower triangular, with diagonal entries from 1 to 2.
All inputs are finite; a program needn't handle non-finite values. No bound on the sum of `mask1` or of `mask2` on one device may be relied on, other than what follows from the above.
Results may differ from a plain program's by a relative error of at most 0.000071.
Values sent between devices are 32-bit elements; how exact they have to be, the bound alone decides.
No kernel may reach another device: no remote copies, remote signals or barrier semaphores. Data moves between devices by JAX's collectives and lax.ppermute only.
A program may use at most 128 MiB of HBM per device.

v0:
```python
import jax
import jax.numpy as jnp
from jax import lax
from jax.sharding import PartitionSpec as P

B = 256
HIGH = lax.Precision.HIGHEST


def shifted(shard, axis, by):
    length = lax.axis_size(axis)
    return lax.ppermute(shard, axis, [(i, (i + by) % length) for i in range(length)])


def product(form, left, right):
    return jnp.einsum(form, left, right, precision=HIGH)


def select_send(sigma_local, row_blocks, slots):
    own_count = lax.axis_size("own")
    own_here = lax.axis_index("own")
    row_here = lax.axis_index("row")
    rows_here = sigma_local.shape[0] // B
    cols_here = sigma_local.shape[1] // B
    rowlist = row_blocks.reshape(own_count, slots, -1)
    group = own_here * cols_here // rows_here
    want_col = lax.dynamic_index_in_dim(rowlist, group, 2, keepdims=False)
    local_col = want_col - own_here * cols_here
    match = ((local_col >= 0) & (local_col < cols_here)).astype(jnp.int32)
    which = jnp.sum(match * jnp.arange(slots, dtype=jnp.int32)[None, :], axis=1)
    chosen = rowlist[jnp.arange(own_count, dtype=jnp.int32), which]
    chosen_row = (
        lax.dynamic_index_in_dim(chosen, row_here, 1, keepdims=False) - row_here * rows_here
    )
    chosen_col = jnp.clip(
        lax.dynamic_index_in_dim(chosen, group, 1, keepdims=False) - own_here * cols_here,
        0,
        cols_here - 1,
    )
    blocks4 = sigma_local.reshape(rows_here, B, cols_here, B)
    return blocks4[chosen_row, :, chosen_col, :]


def select_take(received, row_blocks, slots, cols_here):
    mine = lax.axis_index("own") * slots + jnp.arange(slots, dtype=jnp.int32)
    rowlist = row_blocks[mine]
    sender = rowlist // cols_here
    return received[sender]


def on_device(
    sigma_anc, row_blocks, panel1, diag_inv1, mask1, parent_block2, panel2, diag_inv2, mask2
):
    slots = panel1.shape[0]
    cols_here = sigma_anc.shape[1] // B
    keep_own2 = mask2.astype(jnp.float32)
    up_parent = product("kij,kjc->kic", parent_block2, diag_inv2)
    factor2_own = keep_own2[:, :, None] * product("kij,kjc->kic", panel2, diag_inv2)
    factor2_child = shifted(factor2_own, "own", -1)
    outgoing = select_send(sigma_anc, row_blocks, slots)
    received = lax.all_to_all(outgoing, "own", split_axis=0, concat_axis=0, tiled=True)
    blocks1 = select_take(received, row_blocks, slots, cols_here)
    keep1 = mask1.astype(jnp.float32)
    factor1 = keep1[:, :, None] * product("kij,kjc->kic", panel1, diag_inv1)
    factors1 = lax.all_gather(factor1, "row", axis=1, tiled=True).reshape(slots, -1, B, B)
    sel1_panel = -keep1[:, :, None] * product("kmij,kmjc->kic", blocks1, factors1)
    gram1 = product("kji,kjc->kic", diag_inv1, diag_inv1)
    sel1_diag = gram1 - lax.psum(product("kji,kjc->kic", factor1, sel1_panel), "row")
    factor2 = keep1[:, :, None] * factor2_child
    factors2 = lax.all_gather(factor2, "row", axis=1, tiled=True).reshape(slots, -1, B, B)
    anc2 = keep1[:, :, None] * product("kmij,kmjc->kic", blocks1, factors2)
    par_panel = shifted(sel1_panel, "own", 1)
    par_anc = shifted(anc2, "own", 1)
    par_diag = shifted(sel1_diag, "own", 1)
    sel2_panel = -keep_own2[:, :, None] * (product("kij,kjc->kic", par_panel, up_parent) + par_anc)
    cross = product("kji,kjc->kic", par_panel, factor2_own)
    back = product("kji,kjc->kic", factor2_own, sel2_panel)
    par_diag, cross, back = lax.optimization_barrier((par_diag, cross, back))
    cross, back = lax.psum((cross, back), "row")
    sel2_parent = -(product("kij,kjc->kic", par_diag, up_parent) + cross)
    gram2 = product("kji,kjc->kic", diag_inv2, diag_inv2)
    sel2_diag = gram2 - product("kji,kjc->kic", up_parent, sel2_parent) - back
    return (sel1_panel, sel1_diag, sel2_parent, sel2_panel, sel2_diag)


def solution(mesh):
    in_specs = (
        P("row", "own"),
        P(),
        P("own", "row", None),
        P("own", None, None),
        P("own", "row"),
        P("own", None, None),
        P("own", "row", None),
        P("own", None, None),
        P("own", "row"),
    )
    out_specs = (
        P("own", "row", None),
        P("own", None, None),
        P("own", None, None),
        P("own", "row", None),
        P("own", None, None),
    )
    return jax.shard_map(
        on_device, mesh=mesh, in_specs=in_specs, out_specs=out_specs, check_vma=False
    )
```

profile of v0, /device:TPU:2, one launch (start us, length us, event | category | flops | bytes accessed | tf_op | source)
XLA Modules:
  0.0 444.9 jit_solution(6164868798614665549)
XLA Ops:
  7.2 0.0 copy-start
  7.2 0.8 copy.67
  8.0 0.1 constant_dynamic-slice_fusion
  8.1 0.1 copy.90
  8.2 0.1 copy.69
  8.3 0.1 fusion.7
  8.5 0.7 gather_fusion
  9.1 5.9 %reshape.167 = f32[8,256,2,256]{3,2,1,0:T(2,128)} reshape(f32[2048,512]{1,0:T(8,128)} %param.9) | data formatting | bytes 8388608 | tf_op jit(solution)/shard_map/reshape | solution.py:40
  15.1 4.7 %copy.72 = f32[8,256,2,256]{3,1,2,0:T(8,128)} copy(f32[8,256,2,256]{3,2,1,0:T(2,128)} %reshape.167) | data formatting | bytes 8388608 | tf_op jit(solution)/shard_map/reshape | solution.py:40
  19.7 0.2 fusion.11
  19.9 6.5 %gather_fusion.1 = f32[32,256,256]{2,1,0:T(8,128)} fusion(f32[8,256,2,256]{3,1,2,0:T(8,128)} %copy.72, s32[32]{0:T(128)S(1)} %fusion.11), kind=kCustom, calls=%fused_computation.1 | custom fusion | bytes 16777472 | tf_op jit(solution)/shard_map/gather | solution.py:41
  26.5 11.8 %all-to-all-start = ((f32[32,256,256]{2,1,0:T(8,128)}), f32[32,256,256]{2,1,0:T(8,128)}, u32[]{:S(2)}, u32[]{:S(2)}) async-start(f32[32,256,256]{2,1,0:T(8,128)} %gather_fusion.1), calls=%async_computation | async-start | bytes 16777216 | tf_op jit(solution)/shard_map/all_to_all | solution.py:61
  38.3 0.0 all-gather.3.cloned.1.call-start
  38.4 1.5 convolution_multiply_fusion.1
  39.8 0.0 all-gather.3.cloned.1.call-update
  39.8 0.0 all-gather.5.cloned.1.call-start
  39.9 0.7 convolution_multiply_fusion
  40.6 2.8 collective-permute-start.2
  43.3 190.9 %collective-permute-done.2 = f32[2,256,256]{2,1,0:T(8,128)S(1)} collective-permute-done((f32[2,256,256]{2,1,0:T(8,128)S(1)}, f32[2,256,256]{2,1,0:T(8,128)S(1)}, u32[]{:S(2)}, u32[]{:S(2)}) %collective-permute-start.2) | collective-permute-done | bytes 524320 | tf_op jit(solution)/shard_map/ppermute | solution.py:12
  234.2 0.9 broadcast_multiply_fusion
  235.1 0.0 all-gather.5.cloned.1.call-update
  235.1 0.0 all-reduce.4.cloned.1.call-start
  235.2 0.6 gather_fusion.2
  235.8 0.1 reshape.158
  235.9 6.2 %gather_fusion.3 = f32[16,256,256]{2,1,0:T(8,128)} fusion(f32[32,256,256]{2,1,0:T(8,128)} %all-to-all-done, s32[1024]{0:T(1024)S(1)} %pad_clamp_fusion), kind=kCustom, calls=%fused_computation.3 | custom fusion | bytes 8388672 | tf_op jit(solution)/shard_map/gather | solution.py:48
  242.1 8.1 %fusion.3 = f32[2,256,256]{2,1,0:T(8,128)S(1)} fusion(f32[2,8,256,256]{3,2,1,0:T(8,128)} %bitcast.67, f32[2,8,256,256]{3,2,1,0:T(8,128)} %bitcast.69, f32[2]{0:T(128)S(1)} %fusion.16), kind=kOutput, calls=%fused_computation.14 | convolution fusion | flops 3221356544 | bytes 8912904 | tf_op jit(solution)/shard_map/kmij,kmjc->kic/dot_general | solution.py:16
  250.2 0.0 copy-start.3
  250.2 0.3 collective-permute-start.1
  250.5 1.9 fusion.18
  252.4 21.4 %all-gather.5.cloned.1.call-done = f32[2,2048,256]{2,1,0:T(8,128)} async-done(((f32[2,256,256]{2,1,0:T(8,128)}), f32[2,2048,256]{2,1,0:T(8,128)}) %all-gather.5.cloned.1.call-update) | async-done | bytes 4194320 | tf_op jit(solution)/shard_map/all_gather | solution.py:70
  273.8 8.2 %fusion.1 = f32[2,256,256]{2,1,0:T(8,128)} fusion(f32[2,8,256,256]{3,2,1,0:T(8,128)} %bitcast.68, f32[2,8,256,256]{3,2,1,0:T(8,128)} %bitcast.70, f32[2]{0:T(128)S(1)} %convert_bitcast_fusion.1), kind=kOutput, calls=%fused_computation.8 | convolution fusion | flops 3221356544 | bytes 8912904 | tf_op jit(solution)/shard_map/kmij,kmjc->kic/dot_general | solution.py:16
  282.0 1.5 collective-permute-start.3
  283.6 0.0 all-reduce.4.cloned.1.call-update
  283.6 0.0 all-reduce.6.cloned.1.call-start
  283.7 1.7 fusion.20
  285.4 63.5 %all-reduce.4.cloned.1.call-done = f32[2,256,256]{2,1,0:T(8,128)} async-done(((f32[2,256,256]{2,1,0:T(8,128)}), f32[2,256,256]{2,1,0:T(8,128)}) %all-reduce.4.cloned.1.call-update) | async-done | bytes 524304 | tf_op jit(solution)/shard_map/psum | solution.py:68
  348.9 2.9 convolution_subtract_fusion.1
  351.8 1.6 collective-permute-start
  353.3 1.7 fusion.2
  355.0 1.8 fusion.21
  356.9 1.8 fusion.19
  358.7 7.1 %collective-permute-done = f32[2,256,256]{2,1,0:T(8,128)} collective-permute-done((f32[2,256,256]{2,1,0:T(8,128)}, f32[2,256,256]{2,1,0:T(8,128)}, u32[]{:S(2)}, u32[]{:S(2)}) %collective-permute-start) | collective-permute-done | bytes 524320 | tf_op jit(solution)/shard_map/ppermute | solution.py:12
  365.8 0.0 all-reduce.6.cloned.1.call-update
  365.8 1.1 fusion.22
  366.9 67.6 %all-reduce.6.cloned.1.call-done = (f32[2,256,256]{2,1,0:T(8,128)}, f32[2,256,256]{2,1,0:T(8,128)}) async-done(((f32[2,256,256]{2,1,0:T(8,128)}, f32[2,256,256]{2,1,0:T(8,128)}), (f32[2,256,256]{2,1,0:T(8,128)}, f32[2,256,256]{2,1,0:T(8,128)})) %all-reduce.6.cloned.1.call-update) | async-done | bytes 1048592 | tf_op jit(solution)/shard_map/psum | solution.py:79
  434.5 1.9 fusion
  436.4 1.0 convolution_subtract_fusion
  437.5 0.9 sub.48
  (33 shorter events, 0.1 us)
Async XLA Ops:
  7.2 32.7 %copy-start = (f32[2,256,256]{2,1,0:T(8,128)S(1)}, f32[2,256,256]{2,1,0:T(8,128)}, u32[]{:S(2)}) copy-start(f32[2,256,256]{2,1,0:T(8,128)} %param.16) | copy-start | bytes 1572868
  26.4 11.9 %copy-start.9 = (s32[2,1]{0,1:T(1,128)S(1)}, s32[2,1]{0,1:T(1,128)}, u32[]{:S(2)}) copy-start(s32[2,1]{0,1:T(1,128)} %param.13) | copy-start | bytes 28
  26.4 11.9 %copy-start.2 = (f32[2,256,256]{2,1,0:T(8,128)S(1)}, f32[2,256,256]{2,1,0:T(8,128)}, u32[]{:S(2)}) copy-start(f32[2,256,256]{2,1,0:T(8,128)} %param.12) | copy-start | bytes 1572868
  26.4 11.9 %copy-start.7 = (f32[2,256,256]{2,1,0:T(8,128)S(1)}, f32[2,256,256]{2,1,0:T(8,128)}, u32[]{:S(2)}) copy-start(f32[2,256,256]{2,1,0:T(8,128)} %param.11) | copy-start | bytes 1572868
  26.4 13.5 %copy-start.10 = (s32[2,1]{0,1:T(1,128)S(1)}, s32[2,1]{0,1:T(1,128)}, u32[]{:S(2)}) copy-start(s32[2,1]{0,1:T(1,128)} %param.17) | copy-start | bytes 28
  26.4 13.5 %copy-start.8 = (f32[2,256,256]{2,1,0:T(8,128)S(1)}, f32[2,256,256]{2,1,0:T(8,128)}, u32[]{:S(2)}) copy-start(f32[2,256,256]{2,1,0:T(8,128)} %param.15) | copy-start | bytes 1572868
  26.5 209.4 %all-to-all-start = ((f32[32,256,256]{2,1,0:T(8,128)}), f32[32,256,256]{2,1,0:T(8,128)}, u32[]{:S(2)}, u32[]{:S(2)}) async-start(f32[32,256,256]{2,1,0:T(8,128)} %gather_fusion.1), calls=%async_computation | async-start | bytes 16777216 | tf_op jit(solution)/shard_map/all_to_all | solution.py:61
  38.3 203.8 %all-gather.3.cloned.1.call-start = ((), (), s32[]{:S(2)}) async-start(), calls=%async_computation.1 | async-start | bytes 4718592 | tf_op jit(solution)/shard_map/all_gather | solution.py:65
  39.8 234.0 %all-gather.5.cloned.1.call-start = ((), (), s32[]{:S(2)}) async-start(), calls=%async_computation.3 | async-start | bytes 4718592 | tf_op jit(solution)/shard_map/all_gather | solution.py:70
  40.6 193.6 %collective-permute-start.2 = (f32[2,256,256]{2,1,0:T(8,128)S(1)}, f32[2,256,256]{2,1,0:T(8,128)S(1)}, u32[]{:S(2)}, u32[]{:S(2)}) collective-permute-start(f32[2,256,256]{2,1,0:T(8,128)S(1)} %convolution_multiply_fusion), channel_id=1, source_target_pairs={{0,248},{8,0},{16,8},{24,16},{32,24},{40,32},{48,40},{56,48},{64,5... | collective-permute-start | bytes 1572872 | tf_op jit(solution)/shard_map/ppermute | solution.py:12
  235.1 113.7 %all-reduce.4.cloned.1.call-start = ((), (), s32[]{:S(2)}) async-start(), calls=%async_computation.2 | async-start | bytes 1048576 | tf_op jit(solution)/shard_map/psum | solution.py:68
  242.1 8.4 %copy-start.1 = (f32[2,256,256]{2,1,0:T(8,128)S(1)}, f32[2,256,256]{2,1,0:T(8,128)}, u32[]{:S(2)}) copy-start(f32[2,256,256]{2,1,0:T(8,128)} %convolution_multiply_fusion.1) | copy-start | bytes 1572868
  250.2 31.8 %copy-start.3 = (f32[2,256,256]{2,1,0:T(8,128)}, f32[2,256,256]{2,1,0:T(8,128)S(1)}, u32[]{:S(2)}) copy-start(f32[2,256,256]{2,1,0:T(8,128)S(1)} %fusion.3) | copy-start | bytes 1572868
  250.2 103.1 %collective-permute-start.1 = (f32[2,256,256]{2,1,0:T(8,128)S(1)}, f32[2,256,256]{2,1,0:T(8,128)S(1)}, u32[]{:S(2)}, u32[]{:S(2)}) collective-permute-start(f32[2,256,256]{2,1,0:T(8,128)S(1)} %fusion.3), channel_id=1, source_target_pairs={{0,8},{8,16},{16,24},{24,32},{32,40},{40,48},{48,56},{56,64},{64,7... | collective-permute-start | bytes 1572872 | tf_op jit(solution)/shard_map/ppermute | solution.py:12
  282.0 71.3 %collective-permute-start.3 = (f32[2,256,256]{2,1,0:T(8,128)}, f32[2,256,256]{2,1,0:T(8,128)}, u32[]{:S(2)}, u32[]{:S(2)}) collective-permute-start(f32[2,256,256]{2,1,0:T(8,128)} %fusion.1), channel_id=1, source_target_pairs={{0,8},{8,16},{16,24},{24,32},{32,40},{40,48},{48,56},{56,64},{64,7... | collective-permute-start | bytes 1572872 | tf_op jit(solution)/shard_map/ppermute | solution.py:12
  283.6 150.9 %all-reduce.6.cloned.1.call-start = ((), (), s32[]{:S(2)}) async-start(), calls=%async_computation.4 | async-start | bytes 2097152 | tf_op jit(solution)/shard_map/psum | solution.py:79
  351.8 14.1 %collective-permute-start = (f32[2,256,256]{2,1,0:T(8,128)}, f32[2,256,256]{2,1,0:T(8,128)}, u32[]{:S(2)}, u32[]{:S(2)}) collective-permute-start(f32[2,256,256]{2,1,0:T(8,128)} %convolution_subtract_fusion.1), channel_id=1, source_target_pairs={{0,8},{8,16},{16,24},{24,32},{32,40},{40,48},{48,56},{56,64},{64,7... | collective-permute-start | bytes 1572872 | tf_op jit(solution)/shard_map/ppermute | solution.py:12
  355.0 82.5 %copy-start.4 = (f32[2,256,256]{2,1,0:T(8,128)}, f32[2,256,256]{2,1,0:T(8,128)S(1)}, u32[]{:S(2)}) copy-start(f32[2,256,256]{2,1,0:T(8,128)S(1)} %fusion.2) | copy-start | bytes 1572868
  434.5 3.0 copy-start.6
  436.4 2.0 copy-start.5
Sparse Core Ops, SparseCore 0:
  41.5 35.7 all-gather.2
  235.3 38.5 all-gather.4
  283.7 65.0 all-reduce.3
  366.0 68.4 all-reduce.5
where the time goes:
time: 445 us
  waiting for transfers between devices  351 us (79%)
  matrix products  34.3 us (8%)
  local copies, waits for them, and re-layouts  25.7 us (6%)
  starting transfers between devices  18.1 us (4%)
  between operations  14 us (3%)
    ppermute x4, waiting for transfers between devices, shifted(): lax.ppermute(shard, axis, [(i, (i + by) % length) for i in range(length)])  198 us
    psum x1, waiting for transfers between devices, on_device(): cross, back = lax.psum((cross, back), 'row')  67.6 us
    psum x1, waiting for transfers between devices, on_device(): lax.psum(product('kji,kjc->kic', factor1, sel1_panel), 'row')  63.5 us
    dot_general x13, matrix products, product(): return jnp.einsum(form, left, right, precision=HIGH)  34.3 us
    all_gather x1, waiting for transfers between devices, on_device(): lax.all_gather(factor2, 'row', axis=1, tiled=True).reshape(slots, -1, B, B)  21.4 us
    all_to_all x1, starting transfers between devices, on_device(): lax.all_to_all(outgoing, 'own', split_axis=0, concat_axis=0, tiled=True)  11.8 us
    reshape x2, local copies, waits for them, and re-layouts, select_send(): blocks4 = sigma_local.reshape(rows_here, B, cols_here, B)  10.6 us
  transfers between devices with their start and end apart: 9, of which 5 were waited for; matrix products, arithmetic and copies ran while one was open for 9% of the time, Pallas kernels for 0%

commit v1 on v0

--- a/solution.py
+++ b/solution.py
@@ -5,6 +5,27 @@
 
 B = 256
 HIGH = lax.Precision.HIGHEST
+
+
+def ring_gather(x, axis, dim):
+    size, index, rows = (lax.axis_size(axis), lax.axis_index(axis), x.shape[dim])
+    right = [(i, (i + 1) % size) for i in range(size)]
+    left = [(i, (i - 1) % size) for i in range(size)]
+    result = jnp.zeros((*x.shape[:dim], size * rows, *x.shape[dim + 1 :]), x.dtype)
+    result = lax.dynamic_update_slice_in_dim(result, x, index * rows, axis=dim)
+    from_left = from_right = x
+    half = size // 2
+    for step in range(1, half + 1):
+        from_left = lax.ppermute(from_left, axis, right)
+        result = lax.dynamic_update_slice_in_dim(
+            result, from_left, (index - step) % size * rows, axis=dim
+        )
+        if step < size - half:
+            from_right = lax.ppermute(from_right, axis, left)
+            result = lax.dynamic_update_slice_in_dim(
+                result, from_right, (index + step) % size * rows, axis=dim
+            )
+    return result
 
 
 def shifted(shard, axis, by):
@@ -67,7 +88,7 @@
     gram1 = product("kji,kjc->kic", diag_inv1, diag_inv1)
     sel1_diag = gram1 - lax.psum(product("kji,kjc->kic", factor1, sel1_panel), "row")
     factor2 = keep1[:, :, None] * factor2_child
-    factors2 = lax.all_gather(factor2, "row", axis=1, tiled=True).reshape(slots, -1, B, B)
+    factors2 = ring_gather(factor2, "row", 1).reshape(slots, -1, B, B)
     anc2 = keep1[:, :, None] * product("kmij,kmjc->kic", blocks1, factors2)
     par_panel = shifted(sel1_panel, "own", 1)
     par_anc = shifted(anc2, "own", 1)

time: 445 us -> 460 us (1.034)
  local copies, waits for them, and re-layouts: 25.7 us -> 37.4 us
  starting transfers between devices: 18.1 us -> 25.3 us
    all_gather x1 -> x0, waiting for transfers between devices: 21.4 us -> none  [on_device(): lax.all_gather(factor2, 'row', axis=1, tiled=True).reshape(slots, -1, B, B)]
    ppermute x0 -> x7, waiting for transfers between devices: none -> 20.9 us  [the longest x4 20.9 us: ring_gather(): from_left = lax.ppermute(from_left, axis, right)]
    dynamic_update_slice x0 -> x7, local copies, waits for them, and re-layouts: none -> 10.1 us  [the longest x4 6.51 us: ring_gather(): lax.dynamic_update_slice_in_dim(result, from_left, (index - step) % size...]
    ppermute x0 -> x7, starting transfers between devices: none -> 8.89 us  [the longest x3 8.88 us: ring_gather(): from_right = lax.ppermute(from_right, axis, left)]
  transfers between devices with their start and end apart: 9 -> 15, of which waited for: 5 -> 8; matrix products, arithmetic and copies ran while one was open for 9% -> 9% of each run, Pallas kernels for 0% -> 0%
where the time goes in v1:
time: 460 us; the launch traced here: 459 us
  waiting for transfers between devices  347 us (75%)
  local copies, waits for them, and re-layouts  37.4 us (8%)
  matrix products  32.2 us (7%)
  starting transfers between devices  25.3 us (6%)
  between operations  14 us (3%)
    ppermute x4, waiting for transfers between devices, shifted(): lax.ppermute(shard, axis, [(i, (i + by) % length) for i in range(length)])  198 us
    psum x1, waiting for transfers between devices, on_device(): cross, back = lax.psum((cross, back), 'row')  67.6 us
    psum x1, waiting for transfers between devices, on_device(): lax.psum(product('kji,kjc->kic', factor1, sel1_panel), 'row')  60.5 us
    dot_general x13, matrix products, product(): return jnp.einsum(form, left, right, precision=HIGH)  32.2 us
    ppermute x4, waiting for transfers between devices, ring_gather(): from_left = lax.ppermute(from_left, axis, right)  20.9 us
    all_to_all x1, starting transfers between devices, on_device(): lax.all_to_all(outgoing, 'own', split_axis=0, concat_axis=0, tiled=True)  11.8 us
    reshape x2, local copies, waits for them, and re-layouts, select_send(): blocks4 = sigma_local.reshape(rows_here, B, cols_here, B)  10.6 us
  transfers between devices with their start and end apart: 15, of which 8 were waited for; matrix products, arithmetic and copies ran while one was open for 9% of the time, Pallas kernels for 0%

profile of v1, /device:TPU:2, one launch (start us, length us, event | category | flops | bytes accessed | tf_op | source)
XLA Modules:
  0.0 459.5 jit_solution(8806912630416945596)
XLA Ops:
  7.2 6.0 %reshape.167 = f32[8,256,2,256]{3,2,1,0:T(2,128)} reshape(f32[2048,512]{1,0:T(8,128)} %param.9) | data formatting | bytes 8388608 | tf_op jit(solution)/shard_map/reshape | solution.py:61
  13.2 4.6 %copy.72 = f32[8,256,2,256]{3,1,2,0:T(8,128)} copy(f32[8,256,2,256]{3,2,1,0:T(2,128)} %reshape.167) | data formatting | bytes 8388608 | tf_op jit(solution)/shard_map/reshape | solution.py:61
  17.9 0.1 constant_dynamic-slice_fusion
  18.2 0.1 fusion.6
  18.4 0.7 gather_fusion
  19.0 0.2 fusion.10
  19.2 6.5 %gather_fusion.1 = f32[32,256,256]{2,1,0:T(8,128)} fusion(f32[8,256,2,256]{3,1,2,0:T(8,128)} %copy.72, s32[32]{0:T(128)S(1)} %fusion.10), kind=kCustom, calls=%fused_computation.1 | custom fusion | bytes 16777472 | tf_op jit(solution)/shard_map/gather | solution.py:62
  25.7 11.8 %all-to-all-start = ((f32[32,256,256]{2,1,0:T(8,128)}), f32[32,256,256]{2,1,0:T(8,128)}, u32[]{:S(2)}, u32[]{:S(2)}) async-start(f32[32,256,256]{2,1,0:T(8,128)} %gather_fusion.1), calls=%async_computation | async-start | bytes 16777216 | tf_op jit(solution)/shard_map/all_to_all | solution.py:82
  37.7 1.5 convolution_multiply_fusion.1
  39.2 0.7 convolution_multiply_fusion
  39.9 2.7 collective-permute-start.2
  42.6 190.9 %collective-permute-done.2 = f32[2,256,256]{2,1,0:T(8,128)S(1)} collective-permute-done((f32[2,256,256]{2,1,0:T(8,128)S(1)}, f32[2,256,256]{2,1,0:T(8,128)S(1)}, u32[]{:S(2)}, u32[]{:S(2)}) %collective-permute-start.2) | collective-permute-done | bytes 524320 | tf_op jit(solution)/shard_map/ppermute | solution.py:33
  233.5 2.3 broadcast_in_dim.5
  235.8 1.1 constant_dynamic-update-slice_fusion.6
  236.9 3.0 collective-permute-start.4
  239.9 7.2 %collective-permute-done.3 = f32[2,256,256]{2,1,0:T(8,128)} collective-permute-done((f32[2,256,256]{2,1,0:T(8,128)}, f32[2,256,256]{2,1,0:T(8,128)}, u32[]{:S(2)}, u32[]{:S(2)}) %collective-permute-start.3) | collective-permute-done | bytes 524320 | tf_op jit(solution)/shard_map/ppermute | solution.py:19
  247.0 0.6 gather_fusion.2
  247.6 3.0 collective-permute-start.6
  250.6 6.6 %collective-permute-done.5 = f32[2,256,256]{2,1,0:T(8,128)} collective-permute-done((f32[2,256,256]{2,1,0:T(8,128)}, f32[2,256,256]{2,1,0:T(8,128)}, u32[]{:S(2)}, u32[]{:S(2)}) %collective-permute-start.5) | collective-permute-done | bytes 524320 | tf_op jit(solution)/shard_map/ppermute | solution.py:19
  257.3 0.7 fusion.19
  257.9 3.0 collective-permute-start.8
  260.9 1.9 constant_dynamic-update-slice_fusion.5
  262.8 4.5 collective-permute-done.7
  267.3 0.8 constant_dynamic-update-slice_fusion.4
  268.1 1.9 constant_dynamic-update-slice_fusion.3
  270.0 1.9 constant_dynamic-update-slice_fusion.2
  271.9 1.9 constant_dynamic-update-slice_fusion.1
  273.8 0.8 constant_dynamic-update-slice_fusion
  274.6 2.7 collective-permute-done.9
  277.3 0.8 constant_dynamic-update-slice_fusion.7
  278.1 6.2 %gather_fusion.3 = f32[16,256,256]{2,1,0:T(8,128)} fusion(f32[32,256,256]{2,1,0:T(8,128)} %all-to-all-done, s32[1024]{0:T(1024)S(1)} %pad_clamp_fusion), kind=kCustom, calls=%fused_computation.3 | custom fusion | bytes 8388672 | tf_op jit(solution)/shard_map/gather | solution.py:69
  284.3 8.1 %fusion.2 = f32[2,256,256]{2,1,0:T(8,128)S(1)} fusion(f32[2,8,256,256]{3,2,1,0:T(8,128)} %bitcast.67, f32[2,8,256,256]{3,2,1,0:T(8,128)} %bitcast.69, f32[2]{0:T(128)S(1)} %fusion.15), kind=kOutput, calls=%fused_computation.12 | convolution fusion | flops 3221356544 | bytes 8912904 | tf_op jit(solution)/shard_map/kmij,kmjc->kic/dot_general | solution.py:37
  292.5 1.9 fusion.17
  294.4 0.2 all-reduce.6.cloned.1.call-start
  294.6 8.2 %fusion.1 = f32[2,256,256]{2,1,0:T(8,128)} fusion(f32[2,8,256,256]{3,2,1,0:T(8,128)} %bitcast.68, f32[2,8,256,256]{3,2,1,0:T(8,128)} %bitcast.11, f32[2]{0:T(128)S(1)} %convert_bitcast_fusion.1), kind=kOutput, calls=%fused_computation.8 | convolution fusion | flops 3221356544 | bytes 8912904 | tf_op jit(solution)/shard_map/kmij,kmjc->kic/dot_general | solution.py:37
  302.9 60.5 %all-reduce.4.cloned.1.call-done = f32[2,256,256]{2,1,0:T(8,128)} async-done(((f32[2,256,256]{2,1,0:T(8,128)}), f32[2,256,256]{2,1,0:T(8,128)}) %all-reduce.4.cloned.1.call-update) | async-done | bytes 524304 | tf_op jit(solution)/shard_map/psum | solution.py:89
  363.4 2.9 convolution_subtract_fusion.1
  366.3 1.6 collective-permute-start
  367.9 0.7 fusion.20
  368.5 1.1 add_multiply_fusion
  369.7 1.8 fusion.21
  371.5 1.8 fusion.18
  373.4 7.0 %collective-permute-done = f32[2,256,256]{2,1,0:T(8,128)} collective-permute-done((f32[2,256,256]{2,1,0:T(8,128)}, f32[2,256,256]{2,1,0:T(8,128)}, u32[]{:S(2)}, u32[]{:S(2)}) %collective-permute-start) | collective-permute-done | bytes 524320 | tf_op jit(solution)/shard_map/ppermute | solution.py:33
  380.4 1.1 fusion.22
  381.5 67.6 %all-reduce.6.cloned.1.call-done = (f32[2,256,256]{2,1,0:T(8,128)}, f32[2,256,256]{2,1,0:T(8,128)}) async-done(((f32[2,256,256]{2,1,0:T(8,128)}, f32[2,256,256]{2,1,0:T(8,128)}), (f32[2,256,256]{2,1,0:T(8,128)}, f32[2,256,256]{2,1,0:T(8,128)})) %all-reduce.6.cloned.1.call-update) | async-done | bytes 1048592 | tf_op jit(solution)/shard_map/psum | solution.py:100
  449.1 1.9 fusion
  451.0 1.0 convolution_subtract_fusion
  452.1 0.9 sub.64
  (57 shorter events, 0.7 us)
Async XLA Ops:
  7.2 32.0 %copy-start = (f32[2,256,256]{2,1,0:T(8,128)S(1)}, f32[2,256,256]{2,1,0:T(8,128)}, u32[]{:S(2)}) copy-start(f32[2,256,256]{2,1,0:T(8,128)} %param.16) | copy-start | bytes 1572868
  13.2 4.6 %copy-start.10 = (s32[64,8]{0,1:T(8,128)S(1)}, s32[64,8]{0,1:T(8,128)}, u32[]{:S(2)}) copy-start(s32[64,8]{0,1:T(8,128)} %param.10) | copy-start | bytes 6148
  25.7 11.9 %copy-start.11 = (s32[2,1]{0,1:T(1,128)S(1)}, s32[2,1]{0,1:T(1,128)}, u32[]{:S(2)}) copy-start(s32[2,1]{0,1:T(1,128)} %param.13) | copy-start | bytes 28
  25.7 11.9 %copy-start.2 = (f32[2,256,256]{2,1,0:T(8,128)S(1)}, f32[2,256,256]{2,1,0:T(8,128)}, u32[]{:S(2)}) copy-start(f32[2,256,256]{2,1,0:T(8,128)} %param.12) | copy-start | bytes 1572868
  25.7 11.9 %copy-start.8 = (f32[2,256,256]{2,1,0:T(8,128)S(1)}, f32[2,256,256]{2,1,0:T(8,128)}, u32[]{:S(2)}) copy-start(f32[2,256,256]{2,1,0:T(8,128)} %param.11) | copy-start | bytes 1572868
  25.7 13.5 %copy-start.12 = (s32[2,1]{0,1:T(1,128)S(1)}, s32[2,1]{0,1:T(1,128)}, u32[]{:S(2)}) copy-start(s32[2,1]{0,1:T(1,128)} %param.17) | copy-start | bytes 28
  25.7 13.5 %copy-start.9 = (f32[2,256,256]{2,1,0:T(8,128)S(1)}, f32[2,256,256]{2,1,0:T(8,128)}, u32[]{:S(2)}) copy-start(f32[2,256,256]{2,1,0:T(8,128)} %param.15) | copy-start | bytes 1572868
  25.7 252.4 %all-to-all-start = ((f32[32,256,256]{2,1,0:T(8,128)}), f32[32,256,256]{2,1,0:T(8,128)}, u32[]{:S(2)}, u32[]{:S(2)}) async-start(f32[32,256,256]{2,1,0:T(8,128)} %gather_fusion.1), calls=%async_computation | async-start | bytes 16777216 | tf_op jit(solution)/shard_map/all_to_all | solution.py:82
  37.6 246.8 %all-gather.2.cloned.1.call-start = ((), (), s32[]{:S(2)}) async-start(), calls=%async_computation.1 | async-start | bytes 4718592 | tf_op jit(solution)/shard_map/all_gather | solution.py:86
  39.1 218.1 %copy-start.6 = (f32[2,256,256]{2,1,0:T(8,128)S(1)}, f32[2,256,256]{2,1,0:T(8,128)}, u32[]{:S(2)}) copy-start(f32[2,256,256]{2,1,0:T(8,128)} %param.14) | copy-start | bytes 1572868
  39.1 324.3 %all-reduce.4.cloned.1.call-start = ((), (), s32[]{:S(2)}) async-start(), calls=%async_computation.2 | async-start | bytes 1048576 | tf_op jit(solution)/shard_map/psum | solution.py:89
  39.9 193.6 %collective-permute-start.2 = (f32[2,256,256]{2,1,0:T(8,128)S(1)}, f32[2,256,256]{2,1,0:T(8,128)S(1)}, u32[]{:S(2)}, u32[]{:S(2)}) collective-permute-start(f32[2,256,256]{2,1,0:T(8,128)S(1)} %convolution_multiply_fusion), channel_id=1, source_target_pairs={{0,248},{8,0},{16,8},{24,16},{32,24},{40,32},{48,40},{56,48},{64,5... | collective-permute-start | bytes 1572872 | tf_op jit(solution)/shard_map/ppermute | solution.py:33
  236.9 10.1 %collective-permute-start.3 = (f32[2,256,256]{2,1,0:T(8,128)}, f32[2,256,256]{2,1,0:T(8,128)}, u32[]{:S(2)}, u32[]{:S(2)}) collective-permute-start(f32[2,256,256]{2,1,0:T(8,128)} %get-tuple-element.14), channel_id=1, source_target_pairs={{0,1},{1,2},{2,3},{3,4},{4,5},{5,6},{6,7},{7,0},{8,9},{9,10},{10,1... | collective-permute-start | bytes 1572872 | tf_op jit(solution)/shard_map/ppermute | solution.py:19
  236.9 10.7 %collective-permute-start.4 = (f32[2,256,256]{2,1,0:T(8,128)}, f32[2,256,256]{2,1,0:T(8,128)S(1)}, u32[]{:S(2)}, u32[]{:S(2)}) collective-permute-start(f32[2,256,256]{2,1,0:T(8,128)} %get-tuple-element.14), channel_id=1, source_target_pairs={{0,7},{1,0},{2,1},{3,2},{4,3},{5,4},{6,5},{7,6},{8,15},{9,8},{10,9... | collective-permute-start | bytes 1572872 | tf_op jit(solution)/shard_map/ppermute | solution.py:24
  247.0 10.1 %collective-permute-start.5 = (f32[2,256,256]{2,1,0:T(8,128)}, f32[2,256,256]{2,1,0:T(8,128)}, u32[]{:S(2)}, u32[]{:S(2)}) collective-permute-start(f32[2,256,256]{2,1,0:T(8,128)} %collective-permute-done.3), channel_id=1, source_target_pairs={{0,1},{1,2},{2,3},{3,4},{4,5},{5,6},{6,7},{7,0},{8,9},{9,10},{10,1... | collective-permute-start | bytes 1572872 | tf_op jit(solution)/shard_map/ppermute | solution.py:19
  247.6 10.3 %collective-permute-start.6 = (f32[2,256,256]{2,1,0:T(8,128)S(1)}, f32[2,256,256]{2,1,0:T(8,128)}, u32[]{:S(2)}, u32[]{:S(2)}) collective-permute-start(f32[2,256,256]{2,1,0:T(8,128)S(1)} %collective-permute-done.4), channel_id=1, source_target_pairs={{0,7},{1,0},{2,1},{3,2},{4,3},{5,4},{6,5},{7,6},{8,15},{9,8},{10,9... | collective-permute-start | bytes 1572872 | tf_op jit(solution)/shard_map/ppermute | solution.py:24
  257.2 10.1 %collective-permute-start.7 = (f32[2,256,256]{2,1,0:T(8,128)}, f32[2,256,256]{2,1,0:T(8,128)}, u32[]{:S(2)}, u32[]{:S(2)}) collective-permute-start(f32[2,256,256]{2,1,0:T(8,128)} %collective-permute-done.5), channel_id=1, source_target_pairs={{0,1},{1,2},{2,3},{3,4},{4,5},{5,6},{6,7},{7,0},{8,9},{9,10},{10,1... | collective-permute-start | bytes 1572872 | tf_op jit(solution)/shard_map/ppermute | solution.py:19
  257.9 15.9 %collective-permute-start.8 = (f32[2,256,256]{2,1,0:T(8,128)}, f32[2,256,256]{2,1,0:T(8,128)S(1)}, u32[]{:S(2)}, u32[]{:S(2)}) collective-permute-start(f32[2,256,256]{2,1,0:T(8,128)} %collective-permute-done.6), channel_id=1, source_target_pairs={{0,7},{1,0},{2,1},{3,2},{4,3},{5,4},{6,5},{7,6},{8,15},{9,8},{10,9... | collective-permute-start | bytes 1572872 | tf_op jit(solution)/shard_map/ppermute | solution.py:24
  267.3 10.0 %collective-permute-start.9 = (f32[2,256,256]{2,1,0:T(8,128)}, f32[2,256,256]{2,1,0:T(8,128)S(1)}, u32[]{:S(2)}, u32[]{:S(2)}) collective-permute-start(f32[2,256,256]{2,1,0:T(8,128)} %collective-permute-done.7), channel_id=1, source_target_pairs={{0,1},{1,2},{2,3},{3,4},{4,5},{5,6},{6,7},{7,0},{8,9},{9,10},{10,1... | collective-permute-start | bytes 1572872 | tf_op jit(solution)/shard_map/ppermute | solution.py:19
  284.3 8.1 %copy-start.1 = (f32[2,256,256]{2,1,0:T(8,128)S(1)}, f32[2,256,256]{2,1,0:T(8,128)}, u32[]{:S(2)}) copy-start(f32[2,256,256]{2,1,0:T(8,128)} %convolution_multiply_fusion.1) | copy-start | bytes 1572868
  292.5 10.4 %copy-start.3 = (f32[2,256,256]{2,1,0:T(8,128)}, f32[2,256,256]{2,1,0:T(8,128)S(1)}, u32[]{:S(2)}) copy-start(f32[2,256,256]{2,1,0:T(8,128)S(1)} %fusion.2) | copy-start | bytes 1572868
  294.4 73.5 %collective-permute-start.1 = (f32[2,256,256]{2,1,0:T(8,128)S(1)}, f32[2,256,256]{2,1,0:T(8,128)S(1)}, u32[]{:S(2)}, u32[]{:S(2)}) collective-permute-start(f32[2,256,256]{2,1,0:T(8,128)S(1)} %fusion.2), channel_id=1, source_target_pairs={{0,8},{8,16},{16,24},{24,32},{32,40},{40,48},{48,56},{56,64},{64,7... | collective-permute-start | bytes 1572872 | tf_op jit(solution)/shard_map/ppermute | solution.py:33
  294.4 154.7 %all-reduce.6.cloned.1.call-start = ((), (), s32[]{:S(2)}) async-start(), calls=%async_computation.3 | async-start | bytes 2097152 | tf_op jit(solution)/shard_map/psum | solution.py:100
  302.9 65.7 %collective-permute-start.10 = (f32[2,256,256]{2,1,0:T(8,128)}, f32[2,256,256]{2,1,0:T(8,128)}, u32[]{:S(2)}, u32[]{:S(2)}) collective-permute-start(f32[2,256,256]{2,1,0:T(8,128)} %fusion.1), channel_id=1, source_target_pairs={{0,8},{8,16},{16,24},{24,32},{32,40},{40,48},{48,56},{56,64},{64,7... | collective-permute-start | bytes 1572872 | tf_op jit(solution)/shard_map/ppermute | solution.py:33
  366.3 14.1 %collective-permute-start = (f32[2,256,256]{2,1,0:T(8,128)}, f32[2,256,256]{2,1,0:T(8,128)}, u32[]{:S(2)}, u32[]{:S(2)}) collective-permute-start(f32[2,256,256]{2,1,0:T(8,128)} %convolution_subtract_fusion.1), channel_id=1, source_target_pairs={{0,8},{8,16},{16,24},{24,32},{32,40},{40,48},{48,56},{56,64},{64,7... | collective-permute-start | bytes 1572872 | tf_op jit(solution)/shard_map/ppermute | solution.py:33
  369.7 82.4 %copy-start.4 = (f32[2,256,256]{2,1,0:T(8,128)}, f32[2,256,256]{2,1,0:T(8,128)S(1)}, u32[]{:S(2)}) copy-start(f32[2,256,256]{2,1,0:T(8,128)S(1)} %add_multiply_fusion) | copy-start | bytes 1572868
  449.1 3.0 copy-start.7
  451.0 2.0 copy-start.5
Sparse Core Ops, SparseCore 0:
  40.8 35.7 all-gather.1
  294.5 68.8 all-reduce.3
  380.5 68.4 all-reduce.5
